TPU v7x, 256 devices: a whole 4x4x8 slice. The times are simulated.
256 devices in a mesh: dp: 8 (over x, core), expert: 32 (over y, z).
Axes of the slice: x: 4, y: 4, z: 8, core: 2. Of those that a mesh axis runs over, the one named last changes fastest.
Arguments:
- tokens: bfloat16 [8192, 2048], P(('dp', 'expert')), may hold values from -6 to 6
- expert_ids: int32 [8192, 8], P(('dp', 'expert')), may hold values from 0 to 31, all different within a row; in each aligned block of 32 rows (0 to 31, 32 to 63, ...) at most 16 rows name the same one
- gate_weights: float32 [8192, 8], P(('dp', 'expert')), may hold values from 0.05 to 0.35
- grad_output: bfloat16 [8192, 2048], P(('dp', 'expert')), may hold values from -6 to 6
- w_gate_up: bfloat16 [32, 2048, 1536], P('expert'), may hold values from -0.125 to 0.125
- w_down: bfloat16 [32, 768, 2048], P('expert'), may hold values from -0.21875 to 0.21875
Outputs:
- mixed: bfloat16 [8192, 2048], P(('dp', 'expert'))
- grad_tokens: bfloat16 [8192, 2048], P(('dp', 'expert'))
- grad_gates: float32 [8192, 8], P(('dp', 'expert'))
- grad_gate_up: float32 [32, 2048, 1536], P('expert', 'dp')
- grad_down: float32 [32, 768, 2048], P('expert', None, 'dp')
Inputs may be any that keep to these rules, and one draw needn't show every extreme that they name: `expert_ids`: in each block of 32 rows (the rows of one device) every expert is named at most 16 times, a bound that some block reaches; a row names 8 different experts, and every expert is named somewhere.
All inputs are finite; a program needn't handle non-finite values.
Results may differ from a plain program's by a relative error of at most 0.015.
Values may be sent and summed in bfloat16 or wider, within the bound.
No kernel may reach another device: no remote copies, remote signals or barrier semaphores. Data moves between devices by JAX's collectives and lax.ppermute only.
A program may use at most 128 MiB of HBM per device.

v0:
```python
import jax
import jax.numpy as jnp
from jax import lax
from jax.sharding import Mesh
from jax.sharding import PartitionSpec as P


def swish_parts(gate_up, hidden_units):
    gate_half = gate_up[..., :hidden_units]
    up_half = gate_up[..., hidden_units:]
    sigmoid_part = jax.nn.sigmoid(gate_half)
    return (gate_half, up_half, sigmoid_part)


def ring_offsets(n):
    half = n // 2
    return list(range(-half, n - half))


def ring_gather(x, axis, n):
    right = [(i, (i + 1) % n) for i in range(n)]
    left = [(i, (i - 1) % n) for i in range(n)]
    half = n // 2
    got = {0: x}
    fwd, bwd = x, x
    for k in range(1, half + 1):
        fwd = lax.ppermute(fwd, axis, right)
        got[-k] = fwd
        if k <= n - half - 1:
            bwd = lax.ppermute(bwd, axis, left)
            got[k] = bwd
    return jax.tree.map(lambda *xs: jnp.stack(xs), *[got[o] for o in ring_offsets(n)])


def ring_reduce(parts, axis, n, send_dtypes):
    right = [(i, (i + 1) % n) for i in range(n)]
    left = [(i, (i - 1) % n) for i in range(n)]
    half = n // 2
    index = {o: i for i, o in enumerate(ring_offsets(n))}

    def pick(o):
        return tuple(p[index[o]] for p in parts)

    def send(acc, perm):
        sent = lax.ppermute(tuple(a.astype(t) for a, t in zip(acc, send_dtypes)), axis, perm)
        return tuple(s.astype(jnp.float32) for s in sent)

    def add(a, b):
        return tuple(x + y for x, y in zip(a, b))

    total = pick(0)
    acc = pick(-half)
    for t in range(1, half):
        acc = add(send(acc, left), pick(-half + t))
    total = add(total, send(acc, left))
    m = n - half - 1
    if m > 0:
        acc = pick(m)
        for t in range(1, m):
            acc = add(send(acc, right), pick(m - t))
        total = add(total, send(acc, right))
    return total


def body(tokens, expert_ids, gate_weights, grad_output, w_gate_up, w_down):
    token_count, top_count = expert_ids.shape
    width = tokens.shape[1]
    per_device = w_gate_up.shape[0]
    hidden_units = w_down.shape[1]
    ny = lax.axis_size("ey")
    nz = lax.axis_size("ez")
    expert_total = ny * nz * per_device
    capacity = min(token_count, 2 * token_count * top_count // expert_total)
    pair_count = token_count * top_count
    my_z = lax.axis_index("ez")

    both_g = ring_gather(jnp.concatenate([tokens, grad_output], axis=1), "ez", nz)
    tok_g = both_g[..., :width]
    dy_g = both_g[..., width:]
    nb = both_g.shape[0]
    half = nz // 2
    meta = jnp.concatenate([expert_ids.astype(jnp.float32), gate_weights], axis=1)
    meta_abs = lax.all_to_all(jnp.broadcast_to(meta[None], (nz,) + meta.shape), "ez", 0, 0, tiled=True)
    meta_g = jnp.take(meta_abs, (my_z + jnp.arange(nz, dtype=jnp.int32) - half) % nz, axis=0)
    ids_g = meta_g[..., :top_count].astype(jnp.int32).reshape(nb, pair_count)
    gates_g = meta_g[..., top_count:].reshape(nb, pair_count)

    dest = (
        (jnp.arange(ny, dtype=jnp.int32)[:, None] * nz + my_z) * per_device
        + jnp.arange(per_device, dtype=jnp.int32)[None, :]
    )
    onehot = ids_g[None, None, :, :] == dest[:, :, None, None]
    onehot_i = onehot.astype(jnp.int32)
    slots = jnp.cumsum(onehot_i, axis=3) - onehot_i
    slot_axis = jnp.arange(capacity, dtype=jnp.int32)
    sel = jnp.logical_and(onehot[:, :, :, None, :], slots[:, :, :, None, :] == slot_axis[:, None])
    sel_f = sel.astype(jnp.float32)
    row_gate = jnp.sum(sel_f * gates_g[None, None, :, None, :], axis=4)
    sel_tok = jnp.sum(
        sel.reshape(ny, per_device, nb, capacity, token_count, top_count).astype(jnp.bfloat16),
        axis=5,
    )
    send_x = jnp.einsum(
        "yjoct,otd->yjocd", sel_tok, tok_g, preferred_element_type=jnp.float32
    ).astype(jnp.bfloat16)
    routed_dy = jnp.einsum("yjoct,otd->yjocd", sel_tok, dy_g, preferred_element_type=jnp.float32)
    send_g = (row_gate[..., None] * routed_dy).astype(jnp.bfloat16)

    def to_rows(a):
        return a.transpose(1, 0, 2, 3, 4).reshape(per_device, ny * nb * capacity, width)

    def from_rows(a):
        return a.reshape(per_device, ny, nb, capacity, width).transpose(1, 0, 2, 3, 4)

    x_rows = to_rows(lax.all_to_all(send_x, "ey", 0, 0, tiled=True))
    gate_up = jnp.einsum("jrd,jdf->jrf", x_rows, w_gate_up, preferred_element_type=jnp.float32)
    gate_half, up_half, sigmoid_part = swish_parts(gate_up, hidden_units)
    swish = gate_half * sigmoid_part
    hidden = (swish * up_half).astype(jnp.bfloat16)
    out_rows = jnp.einsum(
        "jrf,jfd->jrd", hidden, w_down, preferred_element_type=jnp.float32
    ).astype(jnp.bfloat16)
    back_out = lax.all_to_all(from_rows(out_rows), "ey", 0, 0, tiled=True)

    grad_rows = to_rows(lax.all_to_all(send_g, "ey", 0, 0, tiled=True))
    grad_hidden = jnp.einsum("jrd,jfd->jrf", grad_rows, w_down, preferred_element_type=jnp.float32)
    grad_gate = grad_hidden * up_half * sigmoid_part * (1.0 + gate_half * (1.0 - sigmoid_part))
    grad_up = grad_hidden * swish
    grad_act = jnp.concatenate([grad_gate, grad_up], axis=2).astype(jnp.bfloat16)
    grad_in = jnp.einsum(
        "jrf,jdf->jrd", grad_act, w_gate_up, preferred_element_type=jnp.float32
    ).astype(jnp.bfloat16)
    back_in = lax.all_to_all(from_rows(grad_in), "ey", 0, 0, tiled=True)

    back_f = back_out.astype(jnp.float32)
    row_inner = jnp.sum(back_f * routed_dy, axis=4)
    gate_part = jnp.sum(sel_f * row_inner[..., None], axis=(0, 1, 3)).reshape(nb, token_count, top_count)
    mixed_part = jnp.einsum(
        "yjoct,yjocd->otd",
        sel_tok.astype(jnp.float32),
        row_gate[..., None] * back_f,
        precision=lax.Precision.HIGHEST,
        preferred_element_type=jnp.float32,
    )
    gate_abs = jnp.take(gate_part, (jnp.arange(nz, dtype=jnp.int32) - my_z + half) % nz, axis=0)
    grad_gates = jnp.sum(lax.all_to_all(gate_abs, "ez", 0, 0, tiled=True), axis=0)
    tokens_part = jnp.einsum("yjoct,yjocd->otd", sel_tok, back_in, preferred_element_type=jnp.float32)
    (both,) = ring_reduce(
        (jnp.concatenate([mixed_part, tokens_part], axis=2),), "ez", nz, (jnp.bfloat16,)
    )
    mixed = both[:, :width]
    grad_tokens = both[:, width:]

    down_local = jnp.einsum("jrf,jrd->jfd", hidden, grad_rows, preferred_element_type=jnp.float32)
    gate_up_local = jnp.einsum("jrd,jrf->jdf", x_rows, grad_act, preferred_element_type=jnp.float32)
    grad_gate_up = lax.psum_scatter(
        gate_up_local.astype(jnp.bfloat16), "dp", scatter_dimension=1, tiled=True
    ).astype(jnp.float32)
    grad_down = lax.psum_scatter(
        down_local.astype(jnp.bfloat16), "dp", scatter_dimension=2, tiled=True
    ).astype(jnp.float32)
    return (
        mixed.astype(jnp.bfloat16),
        grad_tokens.astype(jnp.bfloat16),
        grad_gates,
        grad_gate_up,
        grad_down,
    )


def solution(mesh):
    ny = mesh.devices.shape[1] // 8 if mesh.devices.shape[1] % 8 == 0 else 1
    nz = mesh.devices.shape[1] // ny
    split = Mesh(mesh.devices.reshape(mesh.devices.shape[0], ny, nz), ("dp", "ey", "ez"))
    rows = ("dp", "ey", "ez")
    experts = ("ey", "ez")
    in_specs = (
        P(rows, None),
        P(rows, None),
        P(rows, None),
        P(rows, None),
        P(experts, None, None),
        P(experts, None, None),
    )
    out_specs = (
        P(rows, None),
        P(rows, None),
        P(rows, None),
        P(experts, "dp", None),
        P(experts, None, "dp"),
    )
    return jax.shard_map(body, mesh=split, in_specs=in_specs, out_specs=out_specs, check_vma=False)
```

profile of v0, /device:TPU:2, one launch (start us, length us, event | category | flops | bytes accessed | tf_op | source)
XLA Modules:
  0.0 261.8 jit_solution(905102192643604448)
XLA Ops:
  12.4 3.9 %collective-permute-start.4 = (bf16[32,4096]{1,0:T(8,128)(2,1)}, bf16[32,4096]{1,0:T(8,128)(2,1)}, u32[]{:S(2)}, u32[]{:S(2)}) collective-permute-start(bf16[32,4096]{1,0:T(8,128)(2,1)} %constant_dynamic-update-slice_fusion), channel_id=1, source_target_pairs={{0,7},{1,0},{2,1},{3,2},{4,3},{5,4},{6,5},{7,6},{8,15},{9,8},{10,9... | collective-permute-start | bytes 786440 | tf_op jit(solution)/shard_map/ppermute | solution.py:30
  18.4 5.8 %all-to-all-start = ((f32[8,1,512]{2,1,0:T(1,128)}), f32[8,1,512]{2,1,0:T(1,128)S(1)}, u32[]{:S(2)}, u32[]{:S(2)}) async-start(f32[8,1,512]{2,1,0:T(1,128)} %reshape.370), calls=%async_computation | async-start | bytes 32768 | tf_op jit(solution)/shard_map/all_to_all | solution.py:83
  24.3 7.7 %all-to-all-done = f32[8,1,512]{2,1,0:T(1,128)S(1)} async-done(((f32[8,1,512]{2,1,0:T(1,128)}), f32[8,1,512]{2,1,0:T(1,128)S(1)}, u32[]{:S(2)}, u32[]{:S(2)}) %all-to-all-start) | async-done | bytes 16416 | tf_op jit(solution)/shard_map/all_to_all | solution.py:83
  35.0 2.3 reduce-window.6
  37.4 4.5 %collective-permute-done.1 = bf16[32,4096]{1,0:T(8,128)(2,1)} collective-permute-done((bf16[32,4096]{1,0:T(8,128)(2,1)}, bf16[32,4096]{1,0:T(8,128)(2,1)}, u32[]{:S(2)}, u32[]{:S(2)}) %collective-permute-start.1) | collective-permute-done | bytes 262176 | tf_op jit(solution)/shard_map/ppermute | solution.py:27
  44.6 3.3 %collective-permute-start.5 = (bf16[32,4096]{1,0:T(8,128)(2,1)}, bf16[32,4096]{1,0:T(8,128)(2,1)S(1)}, u32[]{:S(2)}, u32[]{:S(2)}) collective-permute-start(bf16[32,4096]{1,0:T(8,128)(2,1)} %collective-permute-done.4), channel_id=1, source_target_pairs={{0,7},{1,0},{2,1},{3,2},{4,3},{5,4},{6,5},{7,6},{8,15},{9,8},{10,9... | collective-permute-start | bytes 786440 | tf_op jit(solution)/shard_map/ppermute | solution.py:30
  47.9 2.3 collective-permute-done.2
  53.0 3.6 %collective-permute-start.6 = (bf16[32,4096]{1,0:T(8,128)(2,1)S(1)}, bf16[32,4096]{1,0:T(8,128)(2,1)S(1)}, u32[]{:S(2)}, u32[]{:S(2)}) collective-permute-start(bf16[32,4096]{1,0:T(8,128)(2,1)S(1)} %collective-permute-done.5), channel_id=1, source_target_pairs={{0,7},{1,0},{2,1},{3,2},{4,3},{5,4},{6,5},{7,6},{8,15},{9,8},{10,9... | collective-permute-start | bytes 786440 | tf_op jit(solution)/shard_map/ppermute | solution.py:30
  65.2 25.4 %all_to_all.30 = bf16[4,1,8,16,2048]{4,3,2,1,0:T(8,128)(2,1)S(1)} all-to-all(bf16[4,1,8,16,2048]{4,3,2,1,0:T(8,128)(2,1)S(1)} %copy.83), channel_id=1, replica_groups=mesh['dp'=8,'ey'=4,'ez'=8] {'ey'}, dimensions={0} | all-to-all | bytes 4194304 | tf_op jit(solution)/shard_map/all_to_all | solution.py:115
  90.6 3.4 %fusion.11 = f32[1,512,1536]{2,1,0:T(8,128)S(1)} fusion(bf16[512,2048]{1,0:T(8,128)(2,1)S(1)} %bitcast.174, bf16[1,2048,1536]{2,1,0:T(8,128)(2,1)S(1)} %bitcast.182), kind=kOutput, calls=%fused_computation.31 | convolution fusion | flops 3221225472 | bytes 11534336 | tf_op jit(solution)/shard_map/jrd,jdf->jrf/dot_general | solution.py:116
  94.6 3.2 %fusion.18 = bf16[512,2048]{1,0:T(8,128)(2,1)} fusion(bf16[512,768]{1,0:T(8,128)(2,1)S(1)} %fusion.39, bf16[1,768,2048]{2,1,0:T(8,128)(2,1)S(1)} %copy-done), kind=kOutput, calls=%fused_computation.37 | convolution fusion | flops 1611661312 | bytes 6029312 | tf_op jit(solution)/shard_map/jrf,jfd->jrd/dot_general | solution.py:120
  97.8 4.4 %all-to-all-start.2 = ((bf16[4,1,8,16,2048]{4,3,2,1,0:T(8,128)(2,1)}), bf16[4,1,8,16,2048]{4,3,2,1,0:T(8,128)(2,1)}, u32[]{:S(2)}, u32[]{:S(2)}) async-start(bf16[4,1,8,16,2048]{4,3,2,1,0:T(8,128)(2,1)} %bitcast.176), calls=%async_computation.2 | async-start | bytes 4194304 | tf_op jit(solution)/shard_map/all_to_all | solution.py:123
  102.8 19.3 %all-to-all-done.2 = bf16[4,1,8,16,2048]{4,3,2,1,0:T(8,128)(2,1)} async-done(((bf16[4,1,8,16,2048]{4,3,2,1,0:T(8,128)(2,1)}), bf16[4,1,8,16,2048]{4,3,2,1,0:T(8,128)(2,1)}, u32[]{:S(2)}, u32[]{:S(2)}) %all-to-all-start.2) | async-done | bytes 2097184 | tf_op jit(solution)/shard_map/all_to_all | solution.py:123
  122.1 2.7 %fusion.6 = (f32[4,8,16]{2,0,1:T(4,128)S(1)}, f32[8,2048,4,16]{1,3,2,0:T(8,128)S(1)}) fusion(bf16[4,1,8,16,2048]{4,3,2,1,0:T(8,128)(2,1)} %all-to-all-done.2, bf16[4,8,16,32]{3,2,1,0:T(8,128)(2,1)S(1)} %fusion.37, bf16[8,32,4096]{2,1,0:T(8,128)(2,1)} %copy-done.5), kind=kOutput, calls=%fused_computation.24 | convolution fusion | flops 70254080 | bytes 7374848 | tf_op jit(solution)/shard_map/yjoct,otd->yjocd/dot_general | solution.py:106
  125.1 4.7 %fusion.8 = (bf16[4,1,8,16,2048]{4,3,0,2,1:T(8,128)(2,1)S(1)}, f32[4,8,16,2048]{3,2,0,1:T(8,128)}) fusion(f32[8,2048,4,16]{1,3,2,0:T(8,128)S(1)} %get-tuple-element.39, f32[4,8,16]{2,0,1:T(4,128)S(1)} %copy.81, bf16[4,1,8,16,2048]{4,3,2,1,0:T(8,128)(2,1)} %all-to-all-done.2), kind=kLoop, calls=%fused_computation.27 | loop fusion | flops 4194304 | bytes 12584960 | tf_op jit(solution)/shard_map/convert_element_type | solution.py:107
  130.1 21.2 %all_to_all.31 = bf16[4,1,8,16,2048]{4,3,2,1,0:T(8,128)(2,1)S(1)} all-to-all(bf16[4,1,8,16,2048]{4,3,2,1,0:T(8,128)(2,1)S(1)} %copy.88), channel_id=1, replica_groups=mesh['dp'=8,'ey'=4,'ez'=8] {'ey'}, dimensions={0} | all-to-all | bytes 4194304 | tf_op jit(solution)/shard_map/all_to_all | solution.py:125
  152.6 3.6 %fusion.24 = bf16[1,768,2048]{2,1,0:T(8,128)(2,1)} fusion(bf16[512,768]{1,0:T(8,128)(2,1)S(1)} %copy-done.10, bf16[512,2048]{1,0:T(8,128)(2,1)S(1)} %bitcast.177), kind=kOutput, calls=%fused_computation.39 | convolution fusion | flops 1612185600 | bytes 6029312 | tf_op jit(solution)/shard_map/jrf,jrd->jfd/dot_general | solution.py:154
  156.5 4.9 %fusion.41 = (bf16[512,768]{1,0:T(8,128)(2,1)S(1)}, bf16[512,768]{1,0:T(8,128)(2,1)S(1)}) fusion(f32[1,512,1536]{2,1,0:T(8,128)} %copy-done.4, bf16[512,2048]{1,0:T(8,128)(2,1)} %bitcast.178, bf16[1,768,2048]{2,1,0:T(8,128)(2,1)S(1)} %copy-done), kind=kOutput, calls=%fused_computation.63 | convolution fusion | flops 1615724544 | bytes 9961472 | tf_op jit(solution)/shard_map/jrd,jfd->jrf/dot_general | solution.py:126
  162.5 5.5 %fusion = bf16[1,2048,1536]{2,1,0:T(8,128)(2,1)} fusion(bf16[512,2048]{1,0:T(8,128)(2,1)S(1)} %bitcast.175, bf16[512,768]{1,0:T(8,128)(2,1)S(1)} %get-tuple-element.27, bf16[512,768]{1,0:T(8,128)(2,1)S(1)} %get-tuple-element.26), kind=kOutput, calls=%fused_computation.16 | convolution fusion | flops 3227516928 | bytes 9961472 | tf_op jit(solution)/shard_map/jrd,jrf->jdf/dot_general | solution.py:155
  169.5 7.6 %fusion.21 = bf16[512,2048]{1,0:T(8,128)(2,1)} fusion(bf16[1,2048,1536]{2,1,0:T(8,128)(2,1)} %param.10, bf16[512,768]{1,0:T(8,128)(2,1)S(1)} %copy-done.14, bf16[512,768]{1,0:T(8,128)(2,1)S(1)} %copy-done.12), kind=kOutput, calls=%fused_computation.38 | convolution fusion | flops 3225419776 | bytes 9961472 | tf_op jit(solution)/shard_map/jrf,jdf->jrd/dot_general | solution.py:130
  177.0 4.5 %all-to-all-start.4 = ((bf16[4,1,8,16,2048]{4,3,2,1,0:T(8,128)(2,1)}), bf16[4,1,8,16,2048]{4,3,2,1,0:T(8,128)(2,1)}, u32[]{:S(2)}, u32[]{:S(2)}) async-start(bf16[4,1,8,16,2048]{4,3,2,1,0:T(8,128)(2,1)} %bitcast.35), calls=%async_computation.4 | async-start | bytes 4194304 | tf_op jit(solution)/shard_map/all_to_all | solution.py:133
  181.5 3.8 %fusion.26 = f32[8,32,2048]{2,1,0:T(8,128)S(1)} fusion(bf16[4,8,16,32]{3,2,1,0:T(8,128)(2,1)S(1)} %fusion.37, f32[4,8,16,2048]{3,2,0,1:T(8,128)} %get-tuple-element.37), kind=kOutput, calls=%fused_computation.41 | convolution fusion | flops 402653184 | bytes 6324224 | tf_op jit(solution)/shard_map/yjoct,yjocd->otd/dot_general | solution.py:138
  185.3 13.9 %all-to-all-done.4 = bf16[4,1,8,16,2048]{4,3,2,1,0:T(8,128)(2,1)} async-done(((bf16[4,1,8,16,2048]{4,3,2,1,0:T(8,128)(2,1)}), bf16[4,1,8,16,2048]{4,3,2,1,0:T(8,128)(2,1)}, u32[]{:S(2)}, u32[]{:S(2)}) %all-to-all-start.4) | async-done | bytes 2097184 | tf_op jit(solution)/shard_map/all_to_all | solution.py:133
  199.2 2.1 convolution_bitcast_fusion
  202.7 8.1 %collective-permute-done.7 = bf16[32,4096]{1,0:T(8,128)(2,1)S(1)} collective-permute-done((bf16[32,4096]{1,0:T(8,128)(2,1)S(1)}, bf16[32,4096]{1,0:T(8,128)(2,1)S(1)}, u32[]{:S(2)}, u32[]{:S(2)}) %collective-permute-start.7) | collective-permute-done | bytes 262176 | tf_op jit(solution)/shard_map/ppermute | solution.py:45
  211.0 2.0 collective-permute-start.11
  213.0 6.5 %collective-permute-done.8 = bf16[32,4096]{1,0:T(8,128)(2,1)S(1)} collective-permute-done((bf16[32,4096]{1,0:T(8,128)(2,1)S(1)}, bf16[32,4096]{1,0:T(8,128)(2,1)S(1)}, u32[]{:S(2)}, u32[]{:S(2)}) %collective-permute-start.8) | collective-permute-done | bytes 262176 | tf_op jit(solution)/shard_map/ppermute | solution.py:45
  220.6 5.3 %collective-permute-done.9 = bf16[32,4096]{1,0:T(8,128)(2,1)S(1)} collective-permute-done((bf16[32,4096]{1,0:T(8,128)(2,1)S(1)}, bf16[32,4096]{1,0:T(8,128)(2,1)S(1)}, u32[]{:S(2)}, u32[]{:S(2)}) %collective-permute-start.9) | collective-permute-done | bytes 262176 | tf_op jit(solution)/shard_map/ppermute | solution.py:45
  226.9 3.2 %collective-permute-start.10 = (bf16[32,4096]{1,0:T(8,128)(2,1)S(1)}, bf16[32,4096]{1,0:T(8,128)(2,1)S(1)}, u32[]{:S(2)}, u32[]{:S(2)}) collective-permute-start(bf16[32,4096]{1,0:T(8,128)(2,1)S(1)} %get-tuple-element.28), channel_id=1, source_target_pairs={{0,7},{1,0},{2,1},{3,2},{4,3},{5,4},{6,5},{7,6},{8,15},{9,8},{10,9... | collective-permute-start | bytes 786440 | tf_op jit(solution)/shard_map/ppermute | solution.py:45
  230.1 3.6 %collective-permute-done.12 = bf16[32,4096]{1,0:T(8,128)(2,1)S(1)} collective-permute-done((bf16[32,4096]{1,0:T(8,128)(2,1)S(1)}, bf16[32,4096]{1,0:T(8,128)(2,1)S(1)}, u32[]{:S(2)}, u32[]{:S(2)}) %collective-permute-start.12) | collective-permute-done | bytes 262176 | tf_op jit(solution)/shard_map/ppermute | solution.py:45
  235.1 12.0 %all_to_all.32 = f32[8,1,256]{2,1,0:T(1,128)S(1)} all-to-all(f32[8,1,256]{2,1,0:T(1,128)S(1)} %reshape.372), channel_id=1, replica_groups=mesh['dp'=8,'ey'=4,'ez'=8] {'ez'}, dimensions={0} | all-to-all | bytes 16384 | tf_op jit(solution)/shard_map/all_to_all | solution.py:146
  252.5 2.5 convert_element_type.168
  (129 shorter events, 40.4 us)
Async XLA Ops:
  7.2 87.4 %copy-start = (bf16[1,768,2048]{2,1,0:T(8,128)(2,1)S(1)}, bf16[1,768,2048]{2,1,0:T(8,128)(2,1)}, u32[]{:S(2)}) copy-start(bf16[1,768,2048]{2,1,0:T(8,128)(2,1)} %param.11) | copy-start | bytes 9437188
  10.5 23.5 %collective-permute-start = (bf16[32,4096]{1,0:T(8,128)(2,1)}, bf16[32,4096]{1,0:T(8,128)(2,1)}, u32[]{:S(2)}, u32[]{:S(2)}) collective-permute-start(bf16[32,4096]{1,0:T(8,128)(2,1)} %constant_dynamic-update-slice_fusion), channel_id=1, source_target_pairs={{0,1},{1,2},{2,3},{3,4},{4,5},{5,6},{6,7},{7,0},{8,9},{9,10},{10,1... | collective-permute-start | bytes 786440 | tf_op jit(solution)/shard_map/ppermute | solution.py:27
  12.4 32.2 %collective-permute-start.4 = (bf16[32,4096]{1,0:T(8,128)(2,1)}, bf16[32,4096]{1,0:T(8,128)(2,1)}, u32[]{:S(2)}, u32[]{:S(2)}) collective-permute-start(bf16[32,4096]{1,0:T(8,128)(2,1)} %constant_dynamic-update-slice_fusion), channel_id=1, source_target_pairs={{0,7},{1,0},{2,1},{3,2},{4,3},{5,4},{6,5},{7,6},{8,15},{9,8},{10,9... | collective-permute-start | bytes 786440 | tf_op jit(solution)/shard_map/ppermute | solution.py:30
  18.4 13.6 %all-to-all-start = ((f32[8,1,512]{2,1,0:T(1,128)}), f32[8,1,512]{2,1,0:T(1,128)S(1)}, u32[]{:S(2)}, u32[]{:S(2)}) async-start(f32[8,1,512]{2,1,0:T(1,128)} %reshape.370), calls=%async_computation | async-start | bytes 32768 | tf_op jit(solution)/shard_map/all_to_all | solution.py:83
  34.0 8.0 %collective-permute-start.1 = (bf16[32,4096]{1,0:T(8,128)(2,1)}, bf16[32,4096]{1,0:T(8,128)(2,1)}, u32[]{:S(2)}, u32[]{:S(2)}) collective-permute-start(bf16[32,4096]{1,0:T(8,128)(2,1)} %collective-permute-done), channel_id=1, source_target_pairs={{0,1},{1,2},{2,3},{3,4},{4,5},{5,6},{6,7},{7,0},{8,9},{9,10},{10,1... | collective-permute-start | bytes 786440 | tf_op jit(solution)/shard_map/ppermute | solution.py:27
  41.9 8.2 %collective-permute-start.2 = (bf16[32,4096]{1,0:T(8,128)(2,1)}, bf16[32,4096]{1,0:T(8,128)(2,1)}, u32[]{:S(2)}, u32[]{:S(2)}) collective-permute-start(bf16[32,4096]{1,0:T(8,128)(2,1)} %collective-permute-done.1), channel_id=1, source_target_pairs={{0,1},{1,2},{2,3},{3,4},{4,5},{5,6},{6,7},{7,0},{8,9},{9,10},{10,1... | collective-permute-start | bytes 786440 | tf_op jit(solution)/shard_map/ppermute | solution.py:27
  44.6 8.4 %collective-permute-start.5 = (bf16[32,4096]{1,0:T(8,128)(2,1)}, bf16[32,4096]{1,0:T(8,128)(2,1)S(1)}, u32[]{:S(2)}, u32[]{:S(2)}) collective-permute-start(bf16[32,4096]{1,0:T(8,128)(2,1)} %collective-permute-done.4), channel_id=1, source_target_pairs={{0,7},{1,0},{2,1},{3,2},{4,3},{5,4},{6,5},{7,6},{8,15},{9,8},{10,9... | collective-permute-start | bytes 786440 | tf_op jit(solution)/shard_map/ppermute | solution.py:30
  50.2 7.8 %collective-permute-start.3 = (bf16[32,4096]{1,0:T(8,128)(2,1)}, bf16[32,4096]{1,0:T(8,128)(2,1)S(1)}, u32[]{:S(2)}, u32[]{:S(2)}) collective-permute-start(bf16[32,4096]{1,0:T(8,128)(2,1)} %collective-permute-done.2), channel_id=1, source_target_pairs={{0,1},{1,2},{2,3},{3,4},{4,5},{5,6},{6,7},{7,0},{8,9},{9,10},{10,1... | collective-permute-start | bytes 786440 | tf_op jit(solution)/shard_map/ppermute | solution.py:27
  53.0 9.8 %collective-permute-start.6 = (bf16[32,4096]{1,0:T(8,128)(2,1)S(1)}, bf16[32,4096]{1,0:T(8,128)(2,1)S(1)}, u32[]{:S(2)}, u32[]{:S(2)}) collective-permute-start(bf16[32,4096]{1,0:T(8,128)(2,1)S(1)} %collective-permute-done.5), channel_id=1, source_target_pairs={{0,7},{1,0},{2,1},{3,2},{4,3},{5,4},{6,5},{7,6},{8,15},{9,8},{10,9... | collective-permute-start | bytes 786440 | tf_op jit(solution)/shard_map/ppermute | solution.py:30
  62.9 1.3 copy-start.5
  64.3 26.4 %slice-start = ((s8[6291456]{0:T(1024)(128)(4,1)}), s8[4194304]{0:T(1024)(128)(4,1)S(1)}, s32[]{:S(2)}) async-start(s8[6291456]{0:T(1024)(128)(4,1)} %bitcast.181), calls=%async_computation.10 | async-start | bytes 8388608
  64.9 25.7 %slice-start.1 = ((s8[6291456]{0:T(1024)(128)(4,1)}), s8[2097152]{0:T(1024)(128)(4,1)S(1)}, s32[]{:S(2)}) async-start(s8[6291456]{0:T(1024)(128)(4,1)} %bitcast.181), calls=%async_computation.11 | async-start | bytes 4194304
  90.6 3.4 %copy-start.6 = (bf16[4,1,8,16,2048]{4,3,2,1,0:T(8,128)(2,1)}, bf16[4,1,8,16,2048]{4,3,2,1,0:T(8,128)(2,1)S(1)}, u32[]{:S(2)}) copy-start(bf16[4,1,8,16,2048]{4,3,2,1,0:T(8,128)(2,1)S(1)} %all_to_all.30) | copy-start | bytes 6291460
  94.1 3.7 %copy-start.4 = (f32[1,512,1536]{2,1,0:T(8,128)}, f32[1,512,1536]{2,1,0:T(8,128)S(1)}, u32[]{:S(2)}) copy-start(f32[1,512,1536]{2,1,0:T(8,128)S(1)} %fusion.11) | copy-start | bytes 9437188
  94.6 3.2 %copy-start.9 = (bf16[512,768]{1,0:T(8,128)(2,1)}, bf16[512,768]{1,0:T(8,128)(2,1)S(1)}, u32[]{:S(2)}) copy-start(bf16[512,768]{1,0:T(8,128)(2,1)S(1)} %fusion.39) | copy-start | bytes 2359300
  97.8 24.3 %all-to-all-start.2 = ((bf16[4,1,8,16,2048]{4,3,2,1,0:T(8,128)(2,1)}), bf16[4,1,8,16,2048]{4,3,2,1,0:T(8,128)(2,1)}, u32[]{:S(2)}, u32[]{:S(2)}) async-start(bf16[4,1,8,16,2048]{4,3,2,1,0:T(8,128)(2,1)} %bitcast.176), calls=%async_computation.2 | async-start | bytes 4194304 | tf_op jit(solution)/shard_map/all_to_all | solution.py:123
  102.3 148.3 %reduce-scatter.5.cloned.1.call-start = ((), (), s32[]{:S(2)}) async-start(), calls=%async_computation.9 | async-start | bytes 3538944 | tf_op jit(solution)/shard_map/reduce_scatter | solution.py:159
  130.0 22.5 %copy-start.10 = (bf16[512,768]{1,0:T(8,128)(2,1)S(1)}, bf16[512,768]{1,0:T(8,128)(2,1)}, u32[]{:S(2)}) copy-start(bf16[512,768]{1,0:T(8,128)(2,1)} %copy-done.9) | copy-start | bytes 2359300
  156.2 96.2 %reduce-scatter.3.cloned.1.call-start = ((), (), s32[]{:S(2)}) async-start(), calls=%async_computation.8 | async-start | bytes 7077888 | tf_op jit(solution)/shard_map/reduce_scatter | solution.py:156
  156.5 6.0 %copy-start.7 = (bf16[4,1,8,16,2048]{4,3,2,1,0:T(8,128)(2,1)S(1)}, bf16[4,1,8,16,2048]{4,3,2,1,0:T(8,128)(2,1)}, u32[]{:S(2)}) copy-start(bf16[4,1,8,16,2048]{4,3,2,1,0:T(8,128)(2,1)} %copy-done.6) | copy-start | bytes 6291460
  168.1 1.4 copy-start.14
  177.0 22.1 %all-to-all-start.4 = ((bf16[4,1,8,16,2048]{4,3,2,1,0:T(8,128)(2,1)}), bf16[4,1,8,16,2048]{4,3,2,1,0:T(8,128)(2,1)}, u32[]{:S(2)}, u32[]{:S(2)}) async-start(bf16[4,1,8,16,2048]{4,3,2,1,0:T(8,128)(2,1)} %bitcast.35), calls=%async_computation.4 | async-start | bytes 4194304 | tf_op jit(solution)/shard_map/all_to_all | solution.py:133
  185.3 48.5 %copy-start.2 = (f32[8,32,2048]{2,1,0:T(8,128)}, f32[8,32,2048]{2,1,0:T(8,128)S(1)}, u32[]{:S(2)}) copy-start(f32[8,32,2048]{2,1,0:T(8,128)S(1)} %fusion.26) | copy-start | bytes 6291460
  201.2 24.7 %copy-start.3 = (f32[8,32,2048]{2,1,0:T(8,128)}, f32[8,32,2048]{2,1,0:T(8,128)S(1)}, u32[]{:S(2)}) copy-start(f32[8,32,2048]{2,1,0:T(8,128)S(1)} %convolution_bitcast_fusion) | copy-start | bytes 6291460
  201.6 9.2 %collective-permute-start.7 = (bf16[32,4096]{1,0:T(8,128)(2,1)S(1)}, bf16[32,4096]{1,0:T(8,128)(2,1)S(1)}, u32[]{:S(2)}, u32[]{:S(2)}) collective-permute-start(bf16[32,4096]{1,0:T(8,128)(2,1)S(1)} %get-tuple-element.30), channel_id=1, source_target_pairs={{0,7},{1,0},{2,1},{3,2},{4,3},{5,4},{6,5},{7,6},{8,15},{9,8},{10,9... | collective-permute-start | bytes 786440 | tf_op jit(solution)/shard_map/ppermute | solution.py:45
  210.9 8.6 %collective-permute-start.8 = (bf16[32,4096]{1,0:T(8,128)(2,1)S(1)}, bf16[32,4096]{1,0:T(8,128)(2,1)S(1)}, u32[]{:S(2)}, u32[]{:S(2)}) collective-permute-start(bf16[32,4096]{1,0:T(8,128)(2,1)S(1)} %fusion.50), channel_id=1, source_target_pairs={{0,7},{1,0},{2,1},{3,2},{4,3},{5,4},{6,5},{7,6},{8,15},{9,8},{10,9... | collective-permute-start | bytes 786440 | tf_op jit(solution)/shard_map/ppermute | solution.py:45
  211.0 9.6 %collective-permute-start.11 = (bf16[32,4096]{1,0:T(8,128)(2,1)S(1)}, bf16[32,4096]{1,0:T(8,128)(2,1)S(1)}, u32[]{:S(2)}, u32[]{:S(2)}) collective-permute-start(bf16[32,4096]{1,0:T(8,128)(2,1)S(1)} %get-tuple-element.31), channel_id=1, source_target_pairs={{0,1},{1,2},{2,3},{3,4},{4,5},{5,6},{6,7},{7,0},{8,9},{9,10},{10,1... | collective-permute-start | bytes 786440 | tf_op jit(solution)/shard_map/ppermute | solution.py:45
  219.5 6.5 %collective-permute-start.9 = (bf16[32,4096]{1,0:T(8,128)(2,1)S(1)}, bf16[32,4096]{1,0:T(8,128)(2,1)S(1)}, u32[]{:S(2)}, u32[]{:S(2)}) collective-permute-start(bf16[32,4096]{1,0:T(8,128)(2,1)S(1)} %fusion.54), channel_id=1, source_target_pairs={{0,7},{1,0},{2,1},{3,2},{4,3},{5,4},{6,5},{7,6},{8,15},{9,8},{10,9... | collective-permute-start | bytes 786440 | tf_op jit(solution)/shard_map/ppermute | solution.py:45
  226.1 7.7 %collective-permute-start.12 = (bf16[32,4096]{1,0:T(8,128)(2,1)S(1)}, bf16[32,4096]{1,0:T(8,128)(2,1)S(1)}, u32[]{:S(2)}, u32[]{:S(2)}) collective-permute-start(bf16[32,4096]{1,0:T(8,128)(2,1)S(1)} %get-tuple-element.29), channel_id=1, source_target_pairs={{0,1},{1,2},{2,3},{3,4},{4,5},{5,6},{6,7},{7,0},{8,9},{9,10},{10,1... | collective-permute-start | bytes 786440 | tf_op jit(solution)/shard_map/ppermute | solution.py:45
  226.9 21.5 %collective-permute-start.10 = (bf16[32,4096]{1,0:T(8,128)(2,1)S(1)}, bf16[32,4096]{1,0:T(8,128)(2,1)S(1)}, u32[]{:S(2)}, u32[]{:S(2)}) collective-permute-start(bf16[32,4096]{1,0:T(8,128)(2,1)S(1)} %get-tuple-element.28), channel_id=1, source_target_pairs={{0,7},{1,0},{2,1},{3,2},{4,3},{5,4},{6,5},{7,6},{8,15},{9,8},{10,9... | collective-permute-start | bytes 786440 | tf_op jit(solution)/shard_map/ppermute | solution.py:45
  234.7 13.7 %collective-permute-start.13 = (bf16[32,4096]{1,0:T(8,128)(2,1)S(1)}, bf16[32,4096]{1,0:T(8,128)(2,1)}, u32[]{:S(2)}, u32[]{:S(2)}) collective-permute-start(bf16[32,4096]{1,0:T(8,128)(2,1)S(1)} %fusion.66), channel_id=1, source_target_pairs={{0,1},{1,2},{2,3},{3,4},{4,5},{5,6},{6,7},{7,0},{8,9},{9,10},{10,1... | collective-permute-start | bytes 786440 | tf_op jit(solution)/shard_map/ppermute | solution.py:45
  248.5 6.5 %copy-start.1 = (bf16[1,768,2048]{2,1,0:T(8,128)(2,1)S(1)}, bf16[1,768,2048]{2,1,0:T(8,128)(2,1)}, u32[]{:S(2)}) copy-start(bf16[1,768,2048]{2,1,0:T(8,128)(2,1)} %param.11) | copy-start | bytes 9437188
  (4 other events, 4.5 us)
Sparse Core Ops, SparseCore 0:
  156.3 30.4 reduce-scatter.4
  189.4 45.5 reduce-scatter.2
where the time goes:
time: 263 us; the launch traced here: 262 us
  waiting for transfers between devices  75.5 us (29%)
  blocking collectives  58.6 us (22%)
  matrix products  37.4 us (14%)
  starting transfers between devices  35.3 us (13%)
  local copies, waits for them, and re-layouts  20.7 us (8%)
  other arithmetic  19.6 us (7%)
  between operations  14.5 us (6%)
    all_to_all x1, blocking collectives, body(): x_rows = to_rows(lax.all_to_all(send_x, 'ey', 0, 0, tiled=True))  25.4 us
    ppermute x7, waiting for transfers between devices, send(): lax.ppermute(tuple((a.astype(t) for a, t in zip(acc, send_dtypes))), axis...  24.5 us
    all_to_all x1, blocking collectives, body(): grad_rows = to_rows(lax.all_to_all(send_g, 'ey', 0, 0, tiled=True))  21.2 us
    all_to_all x1, waiting for transfers between devices, body(): back_out = lax.all_to_all(from_rows(out_rows), 'ey', 0, 0, tiled=True)  19.3 us
    all_to_all x1, waiting for transfers between devices, body(): back_in = lax.all_to_all(from_rows(grad_in), 'ey', 0, 0, tiled=True)  13.9 us
    unnamed x47, local copies, waits for them, and re-layouts  12.8 us
    all_to_all x1, blocking collectives, body(): lax.all_to_all(gate_abs, 'ez', 0, 0, tiled=True)  12 us
    ppermute x3, starting transfers between devices, ring_gather(): bwd = lax.ppermute(bwd, axis, left)  10.8 us
  transfers between devices with their start and end apart: 19, of which 12 were waited for; matrix products, arithmetic and copies ran while one was open for 18% of the time, Pallas kernels for 0%

commit v1 on v0

--- a/solution.py
+++ b/solution.py
@@ -10,6 +10,19 @@
     up_half = gate_up[..., hidden_units:]
     sigmoid_part = jax.nn.sigmoid(gate_half)
     return (gate_half, up_half, sigmoid_part)
+
+
+def split3(x):
+    hi = x.astype(jnp.bfloat16)
+    rest = x - hi.astype(jnp.float32)
+    mid = rest.astype(jnp.bfloat16)
+    lo = (rest - mid.astype(jnp.float32)).astype(jnp.bfloat16)
+    return [hi, mid, lo]
+
+
+def join3(parts, width):
+    parts = parts.astype(jnp.float32)
+    return (parts[..., :width] + parts[..., width : 2 * width]) + parts[..., 2 * width : 3 * width]
 
 
 def ring_offsets(n):
@@ -74,16 +87,16 @@
     pair_count = token_count * top_count
     my_z = lax.axis_index("ez")
 
-    both_g = ring_gather(jnp.concatenate([tokens, grad_output], axis=1), "ez", nz)
+    packed = jnp.concatenate(
+        [tokens, grad_output, expert_ids.astype(jnp.bfloat16)] + split3(gate_weights), axis=1
+    )
+    both_g = ring_gather(packed, "ez", nz)
     tok_g = both_g[..., :width]
-    dy_g = both_g[..., width:]
+    dy_g = both_g[..., width : 2 * width]
     nb = both_g.shape[0]
-    half = nz // 2
-    meta = jnp.concatenate([expert_ids.astype(jnp.float32), gate_weights], axis=1)
-    meta_abs = lax.all_to_all(jnp.broadcast_to(meta[None], (nz,) + meta.shape), "ez", 0, 0, tiled=True)
-    meta_g = jnp.take(meta_abs, (my_z + jnp.arange(nz, dtype=jnp.int32) - half) % nz, axis=0)
+    meta_g = both_g[..., 2 * width :].astype(jnp.float32)
     ids_g = meta_g[..., :top_count].astype(jnp.int32).reshape(nb, pair_count)
-    gates_g = meta_g[..., top_count:].reshape(nb, pair_count)
+    gates_g = join3(meta_g[..., top_count:], top_count).reshape(nb, pair_count)
 
     dest = (
         (jnp.arange(ny, dtype=jnp.int32)[:, None] * nz + my_z) * per_device
@@ -142,14 +155,14 @@
         precision=lax.Precision.HIGHEST,
         preferred_element_type=jnp.float32,
     )
-    gate_abs = jnp.take(gate_part, (jnp.arange(nz, dtype=jnp.int32) - my_z + half) % nz, axis=0)
-    grad_gates = jnp.sum(lax.all_to_all(gate_abs, "ez", 0, 0, tiled=True), axis=0)
     tokens_part = jnp.einsum("yjoct,yjocd->otd", sel_tok, back_in, preferred_element_type=jnp.float32)
+    gate_parts = [p.astype(jnp.float32) for p in split3(gate_part)]
     (both,) = ring_reduce(
-        (jnp.concatenate([mixed_part, tokens_part], axis=2),), "ez", nz, (jnp.bfloat16,)
+        (jnp.concatenate([mixed_part, tokens_part] + gate_parts, axis=2),), "ez", nz, (jnp.bfloat16,)
     )
     mixed = both[:, :width]
-    grad_tokens = both[:, width:]
+    grad_tokens = both[:, width : 2 * width]
+    grad_gates = join3(both[:, 2 * width :], top_count)
 
     down_local = jnp.einsum("jrf,jrd->jfd", hidden, grad_rows, preferred_element_type=jnp.float32)
     gate_up_local = jnp.einsum("jrd,jrf->jdf", x_rows, grad_act, preferred_element_type=jnp.float32)

time: 263 us -> 265 us (level)
  waiting for transfers between devices: 75.5 us -> 84 us
  blocking collectives: 58.6 us -> 50.6 us
  starting transfers between devices: 35.3 us -> 32.5 us
  matrix products: 37.4 us -> 40.1 us
    ppermute x4, waiting for transfers between devices: 8.12 us -> 25.6 us  [ring_gather(): fwd = lax.ppermute(fwd, axis, right)]
    all_to_all x1 -> x0, blocking collectives: 12 us -> none  [body(): lax.all_to_all(gate_abs, 'ez', 0, 0, tiled=True)]
    all_to_all x1 -> x0, waiting for transfers between devices: 7.71 us -> none  [body(): lax.all_to_all(jnp.broadcast_to(meta[None], (nz,) + meta.shape), 'ez', 0,...]
    all_to_all x1 -> x0, starting transfers between devices: 5.84 us -> none  [body(): lax.all_to_all(jnp.broadcast_to(meta[None], (nz,) + meta.shape), 'ez', 0,...]
    ppermute x7, starting transfers between devices: 6.8 us -> 11.6 us  [send(): lax.ppermute(tuple((a.astype(t) for a, t in zip(acc, send_dtypes))), axis...]
    concatenate x1 -> x2, local copies, waits for them, and re-layouts: 1.57 us -> 5.86 us  [the longest x1 4.79 us: body(): jnp.concatenate([mixed_part, tokens_part] + gate_parts, axis=2)]
    unnamed x47 -> x44, local copies, waits for them, and re-layouts: 12.8 us -> 10.7 us
  transfers between devices with their start and end apart: 19 -> 18, of which waited for: 12 -> 12; matrix products, arithmetic and copies ran while one was open for 18% -> 17% of each run, Pallas kernels for 0% -> 0%
where the time goes in v1:
time: 265 us; the launch traced here: 264 us
  waiting for transfers between devices  84 us (32%)
  blocking collectives  50.6 us (19%)
  matrix products  40.1 us (15%)
  starting transfers between devices  32.5 us (12%)
  local copies, waits for them, and re-layouts  22.9 us (9%)
  other arithmetic  19 us (7%)
  between operations  14.4 us (5%)
    all_to_all x1, blocking collectives, body(): x_rows = to_rows(lax.all_to_all(send_x, 'ey', 0, 0, tiled=True))  27.3 us
    ppermute x4, waiting for transfers between devices, ring_gather(): fwd = lax.ppermute(fwd, axis, right)  25.6 us
    all_to_all x1, blocking collectives, body(): grad_rows = to_rows(lax.all_to_all(send_g, 'ey', 0, 0, tiled=True))  23.4 us
    ppermute x7, waiting for transfers between devices, send(): lax.ppermute(tuple((a.astype(t) for a, t in zip(acc, send_dtypes))), axis...  22 us
    all_to_all x1, waiting for transfers between devices, body(): back_out = lax.all_to_all(from_rows(out_rows), 'ey', 0, 0, tiled=True)  20.7 us
    all_to_all x1, waiting for transfers between devices, body(): back_in = lax.all_to_all(from_rows(grad_in), 'ey', 0, 0, tiled=True)  15.7 us
    ppermute x7, starting transfers between devices, send(): lax.ppermute(tuple((a.astype(t) for a, t in zip(acc, send_dtypes))), axis...  11.6 us
    unnamed x44, local copies, waits for them, and re-layouts  10.7 us
  transfers between devices with their start and end apart: 18, of which 12 were waited for; matrix products, arithmetic and copies ran while one was open for 17% of the time, Pallas kernels for 0%

profile of v1, /device:TPU:2, one launch (start us, length us, event | category | flops | bytes accessed | tf_op | source)
XLA Modules:
  0.0 263.6 jit_solution(10484560744858753953)
XLA Ops:
  12.2 10.4 %collective-permute-done = bf16[32,4128]{1,0:T(8,128)(2,1)S(1)} collective-permute-done((bf16[32,4128]{1,0:T(8,128)(2,1)S(1)}, bf16[32,4128]{1,0:T(8,128)(2,1)S(1)}, u32[]{:S(2)}, u32[]{:S(2)}) %collective-permute-start) | collective-permute-done | bytes 264224 | tf_op jit(solution)/shard_map/ppermute | solution.py:40
  22.6 3.2 %collective-permute-start.4 = (bf16[32,4128]{1,0:T(8,128)(2,1)S(1)}, bf16[32,4128]{1,0:T(8,128)(2,1)}, u32[]{:S(2)}, u32[]{:S(2)}) collective-permute-start(bf16[32,4128]{1,0:T(8,128)(2,1)S(1)} %concatenate.18), channel_id=1, source_target_pairs={{0,7},{1,0},{2,1},{3,2},{4,3},{5,4},{6,5},{7,6},{8,15},{9,8},{10,9... | collective-permute-start | bytes 792584 | tf_op jit(solution)/shard_map/ppermute | solution.py:43
  25.9 5.6 %collective-permute-done.1 = bf16[32,4128]{1,0:T(8,128)(2,1)S(1)} collective-permute-done((bf16[32,4128]{1,0:T(8,128)(2,1)S(1)}, bf16[32,4128]{1,0:T(8,128)(2,1)S(1)}, u32[]{:S(2)}, u32[]{:S(2)}) %collective-permute-start.1) | collective-permute-done | bytes 264224 | tf_op jit(solution)/shard_map/ppermute | solution.py:40
  31.5 3.2 %collective-permute-start.5 = (bf16[32,4128]{1,0:T(8,128)(2,1)}, bf16[32,4128]{1,0:T(8,128)(2,1)}, u32[]{:S(2)}, u32[]{:S(2)}) collective-permute-start(bf16[32,4128]{1,0:T(8,128)(2,1)} %collective-permute-done.4), channel_id=1, source_target_pairs={{0,7},{1,0},{2,1},{3,2},{4,3},{5,4},{6,5},{7,6},{8,15},{9,8},{10,9... | collective-permute-start | bytes 792584 | tf_op jit(solution)/shard_map/ppermute | solution.py:43
  34.7 4.9 %collective-permute-done.2 = bf16[32,4128]{1,0:T(8,128)(2,1)} collective-permute-done((bf16[32,4128]{1,0:T(8,128)(2,1)S(1)}, bf16[32,4128]{1,0:T(8,128)(2,1)}, u32[]{:S(2)}, u32[]{:S(2)}) %collective-permute-start.2) | collective-permute-done | bytes 264224 | tf_op jit(solution)/shard_map/ppermute | solution.py:40
  39.6 3.2 %collective-permute-start.6 = (bf16[32,4128]{1,0:T(8,128)(2,1)}, bf16[32,4128]{1,0:T(8,128)(2,1)S(1)}, u32[]{:S(2)}, u32[]{:S(2)}) collective-permute-start(bf16[32,4128]{1,0:T(8,128)(2,1)} %collective-permute-done.5), channel_id=1, source_target_pairs={{0,7},{1,0},{2,1},{3,2},{4,3},{5,4},{6,5},{7,6},{8,15},{9,8},{10,9... | collective-permute-start | bytes 792584 | tf_op jit(solution)/shard_map/ppermute | solution.py:43
  42.8 4.7 %collective-permute-done.3 = bf16[32,4128]{1,0:T(8,128)(2,1)} collective-permute-done((bf16[32,4128]{1,0:T(8,128)(2,1)}, bf16[32,4128]{1,0:T(8,128)(2,1)}, u32[]{:S(2)}, u32[]{:S(2)}) %collective-permute-start.3) | collective-permute-done | bytes 264224 | tf_op jit(solution)/shard_map/ppermute | solution.py:40
  63.6 27.3 %all_to_all.20 = bf16[4,1,8,16,2048]{4,3,2,1,0:T(8,128)(2,1)S(1)} all-to-all(bf16[4,1,8,16,2048]{4,3,2,1,0:T(8,128)(2,1)S(1)} %copy.86), channel_id=1, replica_groups=mesh['dp'=8,'ey'=4,'ez'=8] {'ey'}, dimensions={0} | all-to-all | bytes 4194304 | tf_op jit(solution)/shard_map/all_to_all | solution.py:128
  90.9 3.4 %fusion.10 = f32[1,512,1536]{2,1,0:T(8,128)S(1)} fusion(bf16[512,2048]{1,0:T(8,128)(2,1)S(1)} %bitcast.163, bf16[1,2048,1536]{2,1,0:T(8,128)(2,1)S(1)} %bitcast.169), kind=kOutput, calls=%fused_computation.15 | convolution fusion | flops 3221225472 | bytes 11534336 | tf_op jit(solution)/shard_map/jrd,jdf->jrf/dot_general | solution.py:129
  94.9 3.2 %fusion.17 = bf16[512,2048]{1,0:T(8,128)(2,1)} fusion(bf16[512,768]{1,0:T(8,128)(2,1)S(1)} %fusion.38, bf16[1,768,2048]{2,1,0:T(8,128)(2,1)S(1)} %copy-done), kind=kOutput, calls=%fused_computation.21 | convolution fusion | flops 1611661312 | bytes 6029312 | tf_op jit(solution)/shard_map/jrf,jfd->jrd/dot_general | solution.py:133
  98.0 4.4 %all-to-all-start.1 = ((bf16[4,1,8,16,2048]{4,3,2,1,0:T(8,128)(2,1)}), bf16[4,1,8,16,2048]{4,3,2,1,0:T(8,128)(2,1)}, u32[]{:S(2)}, u32[]{:S(2)}) async-start(bf16[4,1,8,16,2048]{4,3,2,1,0:T(8,128)(2,1)} %bitcast.165), calls=%async_computation.1 | async-start | bytes 4194304 | tf_op jit(solution)/shard_map/all_to_all | solution.py:136
  103.8 20.7 %all-to-all-done.1 = bf16[4,1,8,16,2048]{4,3,2,1,0:T(8,128)(2,1)} async-done(((bf16[4,1,8,16,2048]{4,3,2,1,0:T(8,128)(2,1)}), bf16[4,1,8,16,2048]{4,3,2,1,0:T(8,128)(2,1)}, u32[]{:S(2)}, u32[]{:S(2)}) %all-to-all-start.1) | async-done | bytes 2097184 | tf_op jit(solution)/shard_map/all_to_all | solution.py:136
  124.5 2.7 %fusion.6 = (f32[4,8,16]{2,0,1:T(4,128)S(1)}, f32[8,2048,4,16]{1,3,2,0:T(8,128)S(1)}) fusion(bf16[4,1,8,16,2048]{4,3,2,1,0:T(8,128)(2,1)} %all-to-all-done.1, bf16[4,8,16,32]{3,2,1,0:T(8,128)(2,1)S(1)} %fusion.36, bf16[8,32,4128]{2,1,0:T(8,128)(2,1)} %copy-done.4), kind=kOutput, calls=%fused_computation.9 | convolution fusion | flops 70254080 | bytes 7374848 | tf_op jit(solution)/shard_map/yjoct,otd->yjocd/dot_general | solution.py:119
  127.5 4.7 %fusion.7 = (bf16[4,1,8,16,2048]{4,3,0,2,1:T(8,128)(2,1)S(1)}, f32[4,8,16,2048]{3,2,0,1:T(8,128)}) fusion(f32[8,2048,4,16]{1,3,2,0:T(8,128)S(1)} %get-tuple-element.59, f32[4,8,16]{2,0,1:T(4,128)S(1)} %copy.84, bf16[4,1,8,16,2048]{4,3,2,1,0:T(8,128)(2,1)} %all-to-all-done.1), kind=kLoop, calls=%fused_computation.11 | loop fusion | flops 4194304 | bytes 12584960 | tf_op jit(solution)/shard_map/convert_element_type | solution.py:120
  132.4 23.4 %all_to_all.21 = bf16[4,1,8,16,2048]{4,3,2,1,0:T(8,128)(2,1)S(1)} all-to-all(bf16[4,1,8,16,2048]{4,3,2,1,0:T(8,128)(2,1)S(1)} %copy.91), channel_id=1, replica_groups=mesh['dp'=8,'ey'=4,'ez'=8] {'ey'}, dimensions={0} | all-to-all | bytes 4194304 | tf_op jit(solution)/shard_map/all_to_all | solution.py:138
  157.1 3.5 %fusion.23 = bf16[1,768,2048]{2,1,0:T(8,128)(2,1)} fusion(bf16[512,768]{1,0:T(8,128)(2,1)S(1)} %copy-done.9, bf16[512,2048]{1,0:T(8,128)(2,1)S(1)} %bitcast.166), kind=kOutput, calls=%fused_computation.23 | convolution fusion | flops 1612185600 | bytes 6029312 | tf_op jit(solution)/shard_map/jrf,jrd->jfd/dot_general | solution.py:167
  160.9 4.9 %fusion.40 = (bf16[512,768]{1,0:T(8,128)(2,1)S(1)}, bf16[512,768]{1,0:T(8,128)(2,1)S(1)}) fusion(f32[1,512,1536]{2,1,0:T(8,128)} %copy-done.3, bf16[512,2048]{1,0:T(8,128)(2,1)} %bitcast.167, bf16[1,768,2048]{2,1,0:T(8,128)(2,1)S(1)} %copy-done), kind=kOutput, calls=%fused_computation.47 | convolution fusion | flops 1615724544 | bytes 9961472 | tf_op jit(solution)/shard_map/jrd,jfd->jrf/dot_general | solution.py:139
  166.9 5.7 %fusion = bf16[1,2048,1536]{2,1,0:T(8,128)(2,1)} fusion(bf16[512,2048]{1,0:T(8,128)(2,1)S(1)} %bitcast.164, bf16[512,768]{1,0:T(8,128)(2,1)S(1)} %get-tuple-element.39, bf16[512,768]{1,0:T(8,128)(2,1)S(1)} %get-tuple-element.38), kind=kOutput, calls=%fused_computation.1 | convolution fusion | flops 3227516928 | bytes 9961472 | tf_op jit(solution)/shard_map/jrd,jrf->jdf/dot_general | solution.py:168
  174.0 7.5 %fusion.20 = bf16[512,2048]{1,0:T(8,128)(2,1)} fusion(bf16[1,2048,1536]{2,1,0:T(8,128)(2,1)} %param.10, bf16[512,768]{1,0:T(8,128)(2,1)S(1)} %copy-done.15, bf16[512,768]{1,0:T(8,128)(2,1)S(1)} %copy-done.13), kind=kOutput, calls=%fused_computation.22 | convolution fusion | flops 3225419776 | bytes 9961472 | tf_op jit(solution)/shard_map/jrf,jdf->jrd/dot_general | solution.py:143
  181.5 4.5 %all-to-all-start.3 = ((bf16[4,1,8,16,2048]{4,3,2,1,0:T(8,128)(2,1)}), bf16[4,1,8,16,2048]{4,3,2,1,0:T(8,128)(2,1)}, u32[]{:S(2)}, u32[]{:S(2)}) async-start(bf16[4,1,8,16,2048]{4,3,2,1,0:T(8,128)(2,1)} %bitcast.34), calls=%async_computation.3 | async-start | bytes 4194304 | tf_op jit(solution)/shard_map/all_to_all | solution.py:146
  186.5 3.8 %fusion.25 = f32[8,32,2048]{2,1,0:T(8,128)S(1)} fusion(bf16[4,8,16,32]{3,2,1,0:T(8,128)(2,1)S(1)} %fusion.36, f32[4,8,16,2048]{3,2,0,1:T(8,128)} %get-tuple-element.54), kind=kOutput, calls=%fused_computation.25 | convolution fusion | flops 402653184 | bytes 6324224 | tf_op jit(solution)/shard_map/yjoct,yjocd->otd/dot_general | solution.py:151
  190.3 15.7 %all-to-all-done.3 = bf16[4,1,8,16,2048]{4,3,2,1,0:T(8,128)(2,1)} async-done(((bf16[4,1,8,16,2048]{4,3,2,1,0:T(8,128)(2,1)}), bf16[4,1,8,16,2048]{4,3,2,1,0:T(8,128)(2,1)}, u32[]{:S(2)}, u32[]{:S(2)}) %all-to-all-start.3) | async-done | bytes 2097184 | tf_op jit(solution)/shard_map/all_to_all | solution.py:146
  206.0 3.5 %convolution_bitcast_fusion = f32[8,32,2048]{2,1,0:T(8,128)} fusion(bf16[4,8,16,32]{3,2,1,0:T(8,128)(2,1)S(1)} %fusion.36, bf16[4,1,8,16,2048]{4,3,2,1,0:T(8,128)(2,1)} %all-to-all-done.3), kind=kOutput, calls=%fused_computation.26 | convolution fusion | flops 67108864 | bytes 4227072 | tf_op jit(solution)/shard_map/yjoct,yjocd->otd/dot_general | solution.py:158
  209.4 4.8 %concatenate.22 = f32[8,32,4120]{2,1,0:T(8,128)} concatenate(f32[8,32,2048]{2,1,0:T(8,128)S(1)} %fusion.25, f32[8,32,2048]{2,1,0:T(8,128)} %convolution_bitcast_fusion, f32[8,32,8]{2,1,0:T(8,128)S(1)} %copy.96, f32[8,32,8]{2,1,0:T(8,128)S(1)} %copy.97, f32[8,32,8]{2,1,0:T(8,128)S(1)} %copy.98), dimensions={2} | concatenate | bytes 8437760 | tf_op jit(solution)/shard_map/concatenate | solution.py:161
  214.2 2.7 %convert.19 = bf16[8,32,4120]{2,1,0:T(8,128)(2,1)S(1)} convert(f32[8,32,4120]{2,1,0:T(8,128)} %concatenate.22) | non-fusion elementwise | flops 1054720 | bytes 6328320 | tf_op jit(solution)/shard_map/convert.4
  219.1 4.4 %collective-permute-done.7 = bf16[32,4120]{1,0:T(8,128)(2,1)S(1)} collective-permute-done((bf16[32,4120]{1,0:T(8,128)(2,1)S(1)}, bf16[32,4120]{1,0:T(8,128)(2,1)S(1)}, u32[]{:S(2)}, u32[]{:S(2)}) %collective-permute-start.7) | collective-permute-done | bytes 263712 | tf_op jit(solution)/shard_map/ppermute | solution.py:58
  223.6 3.6 %collective-permute-start.8 = (bf16[32,4120]{1,0:T(8,128)(2,1)S(1)}, bf16[32,4120]{1,0:T(8,128)(2,1)S(1)}, u32[]{:S(2)}, u32[]{:S(2)}) collective-permute-start(bf16[32,4120]{1,0:T(8,128)(2,1)S(1)} %fusion.50), channel_id=1, source_target_pairs={{0,7},{1,0},{2,1},{3,2},{4,3},{5,4},{6,5},{7,6},{8,15},{9,8},{10,9... | collective-permute-start | bytes 791048 | tf_op jit(solution)/shard_map/ppermute | solution.py:58
  227.2 4.1 %collective-permute-done.8 = bf16[32,4120]{1,0:T(8,128)(2,1)S(1)} collective-permute-done((bf16[32,4120]{1,0:T(8,128)(2,1)S(1)}, bf16[32,4120]{1,0:T(8,128)(2,1)S(1)}, u32[]{:S(2)}, u32[]{:S(2)}) %collective-permute-start.8) | collective-permute-done | bytes 263712 | tf_op jit(solution)/shard_map/ppermute | solution.py:58
  231.4 3.8 %collective-permute-start.9 = (bf16[32,4120]{1,0:T(8,128)(2,1)S(1)}, bf16[32,4120]{1,0:T(8,128)(2,1)S(1)}, u32[]{:S(2)}, u32[]{:S(2)}) collective-permute-start(bf16[32,4120]{1,0:T(8,128)(2,1)S(1)} %get-tuple-element.42), channel_id=1, source_target_pairs={{0,7},{1,0},{2,1},{3,2},{4,3},{5,4},{6,5},{7,6},{8,15},{9,8},{10,9... | collective-permute-start | bytes 791048 | tf_op jit(solution)/shard_map/ppermute | solution.py:58
  235.2 5.0 %collective-permute-done.9 = bf16[32,4120]{1,0:T(8,128)(2,1)S(1)} collective-permute-done((bf16[32,4120]{1,0:T(8,128)(2,1)S(1)}, bf16[32,4120]{1,0:T(8,128)(2,1)S(1)}, u32[]{:S(2)}, u32[]{:S(2)}) %collective-permute-start.9) | collective-permute-done | bytes 263712 | tf_op jit(solution)/shard_map/ppermute | solution.py:58
  240.2 2.6 %collective-permute-done.12 = bf16[32,4120]{1,0:T(8,128)(2,1)S(1)} collective-permute-done((bf16[32,4120]{1,0:T(8,128)(2,1)S(1)}, bf16[32,4120]{1,0:T(8,128)(2,1)S(1)}, u32[]{:S(2)}, u32[]{:S(2)}) %collective-permute-start.12) | collective-permute-done | bytes 263712 | tf_op jit(solution)/shard_map/ppermute | solution.py:58
  245.1 4.4 %collective-permute-done.10 = bf16[32,4120]{1,0:T(8,128)(2,1)S(1)} collective-permute-done((bf16[32,4120]{1,0:T(8,128)(2,1)S(1)}, bf16[32,4120]{1,0:T(8,128)(2,1)S(1)}, u32[]{:S(2)}, u32[]{:S(2)}) %collective-permute-start.10) | collective-permute-done | bytes 263712 | tf_op jit(solution)/shard_map/ppermute | solution.py:58
  (119 shorter events, 39.6 us)
Async XLA Ops:
  7.2 87.7 %copy-start = (bf16[1,768,2048]{2,1,0:T(8,128)(2,1)S(1)}, bf16[1,768,2048]{2,1,0:T(8,128)(2,1)}, u32[]{:S(2)}) copy-start(bf16[1,768,2048]{2,1,0:T(8,128)(2,1)} %param.11) | copy-start | bytes 9437188
  10.2 12.4 %collective-permute-start = (bf16[32,4128]{1,0:T(8,128)(2,1)S(1)}, bf16[32,4128]{1,0:T(8,128)(2,1)S(1)}, u32[]{:S(2)}, u32[]{:S(2)}) collective-permute-start(bf16[32,4128]{1,0:T(8,128)(2,1)S(1)} %concatenate.18), channel_id=1, source_target_pairs={{0,1},{1,2},{2,3},{3,4},{4,5},{5,6},{6,7},{7,0},{8,9},{9,10},{10,1... | collective-permute-start | bytes 792584 | tf_op jit(solution)/shard_map/ppermute | solution.py:40
  22.6 8.9 %copy-start.10 = (bf16[32,4128]{1,0:T(8,128)(2,1)}, bf16[32,4128]{1,0:T(8,128)(2,1)S(1)}, u32[]{:S(2)}) copy-start(bf16[32,4128]{1,0:T(8,128)(2,1)S(1)} %collective-permute-done) | copy-start | bytes 792580
  22.6 8.9 %collective-permute-start.1 = (bf16[32,4128]{1,0:T(8,128)(2,1)S(1)}, bf16[32,4128]{1,0:T(8,128)(2,1)S(1)}, u32[]{:S(2)}, u32[]{:S(2)}) collective-permute-start(bf16[32,4128]{1,0:T(8,128)(2,1)S(1)} %collective-permute-done), channel_id=1, source_target_pairs={{0,1},{1,2},{2,3},{3,4},{4,5},{5,6},{6,7},{7,0},{8,9},{9,10},{10,1... | collective-permute-start | bytes 792584 | tf_op jit(solution)/shard_map/ppermute | solution.py:40
  22.6 8.9 %collective-permute-start.4 = (bf16[32,4128]{1,0:T(8,128)(2,1)S(1)}, bf16[32,4128]{1,0:T(8,128)(2,1)}, u32[]{:S(2)}, u32[]{:S(2)}) collective-permute-start(bf16[32,4128]{1,0:T(8,128)(2,1)S(1)} %concatenate.18), channel_id=1, source_target_pairs={{0,7},{1,0},{2,1},{3,2},{4,3},{5,4},{6,5},{7,6},{8,15},{9,8},{10,9... | collective-permute-start | bytes 792584 | tf_op jit(solution)/shard_map/ppermute | solution.py:43
  31.5 3.2 %copy-start.11 = (bf16[32,4128]{1,0:T(8,128)(2,1)}, bf16[32,4128]{1,0:T(8,128)(2,1)S(1)}, u32[]{:S(2)}) copy-start(bf16[32,4128]{1,0:T(8,128)(2,1)S(1)} %collective-permute-done.1) | copy-start | bytes 792580
  31.5 8.1 %collective-permute-start.2 = (bf16[32,4128]{1,0:T(8,128)(2,1)S(1)}, bf16[32,4128]{1,0:T(8,128)(2,1)}, u32[]{:S(2)}, u32[]{:S(2)}) collective-permute-start(bf16[32,4128]{1,0:T(8,128)(2,1)S(1)} %collective-permute-done.1), channel_id=1, source_target_pairs={{0,1},{1,2},{2,3},{3,4},{4,5},{5,6},{6,7},{7,0},{8,9},{9,10},{10,1... | collective-permute-start | bytes 792584 | tf_op jit(solution)/shard_map/ppermute | solution.py:40
  31.5 8.1 %collective-permute-start.5 = (bf16[32,4128]{1,0:T(8,128)(2,1)}, bf16[32,4128]{1,0:T(8,128)(2,1)}, u32[]{:S(2)}, u32[]{:S(2)}) collective-permute-start(bf16[32,4128]{1,0:T(8,128)(2,1)} %collective-permute-done.4), channel_id=1, source_target_pairs={{0,7},{1,0},{2,1},{3,2},{4,3},{5,4},{6,5},{7,6},{8,15},{9,8},{10,9... | collective-permute-start | bytes 792584 | tf_op jit(solution)/shard_map/ppermute | solution.py:43
  39.6 8.0 %collective-permute-start.3 = (bf16[32,4128]{1,0:T(8,128)(2,1)}, bf16[32,4128]{1,0:T(8,128)(2,1)}, u32[]{:S(2)}, u32[]{:S(2)}) collective-permute-start(bf16[32,4128]{1,0:T(8,128)(2,1)} %collective-permute-done.2), channel_id=1, source_target_pairs={{0,1},{1,2},{2,3},{3,4},{4,5},{5,6},{6,7},{7,0},{8,9},{9,10},{10,1... | collective-permute-start | bytes 792584 | tf_op jit(solution)/shard_map/ppermute | solution.py:40
  39.6 13.9 %collective-permute-start.6 = (bf16[32,4128]{1,0:T(8,128)(2,1)}, bf16[32,4128]{1,0:T(8,128)(2,1)S(1)}, u32[]{:S(2)}, u32[]{:S(2)}) collective-permute-start(bf16[32,4128]{1,0:T(8,128)(2,1)} %collective-permute-done.5), channel_id=1, source_target_pairs={{0,7},{1,0},{2,1},{3,2},{4,3},{5,4},{6,5},{7,6},{8,15},{9,8},{10,9... | collective-permute-start | bytes 792584 | tf_op jit(solution)/shard_map/ppermute | solution.py:43
  53.5 1.4 copy-start.4
  61.3 29.6 %slice-start = ((s8[6291456]{0:T(1024)(128)(4,1)}), s8[4194304]{0:T(1024)(128)(4,1)S(1)}, s32[]{:S(2)}) async-start(s8[6291456]{0:T(1024)(128)(4,1)} %bitcast.168), calls=%async_computation.8 | async-start | bytes 8388608
  63.4 27.6 %slice-start.1 = ((s8[6291456]{0:T(1024)(128)(4,1)}), s8[2097152]{0:T(1024)(128)(4,1)S(1)}, s32[]{:S(2)}) async-start(s8[6291456]{0:T(1024)(128)(4,1)} %bitcast.168), calls=%async_computation.9 | async-start | bytes 4194304
  90.9 3.4 %copy-start.5 = (bf16[4,1,8,16,2048]{4,3,2,1,0:T(8,128)(2,1)}, bf16[4,1,8,16,2048]{4,3,2,1,0:T(8,128)(2,1)S(1)}, u32[]{:S(2)}) copy-start(bf16[4,1,8,16,2048]{4,3,2,1,0:T(8,128)(2,1)S(1)} %all_to_all.20) | copy-start | bytes 6291460
  94.4 3.7 %copy-start.3 = (f32[1,512,1536]{2,1,0:T(8,128)}, f32[1,512,1536]{2,1,0:T(8,128)S(1)}, u32[]{:S(2)}) copy-start(f32[1,512,1536]{2,1,0:T(8,128)S(1)} %fusion.10) | copy-start | bytes 9437188
  94.9 3.2 %copy-start.8 = (bf16[512,768]{1,0:T(8,128)(2,1)}, bf16[512,768]{1,0:T(8,128)(2,1)S(1)}, u32[]{:S(2)}) copy-start(bf16[512,768]{1,0:T(8,128)(2,1)S(1)} %fusion.38) | copy-start | bytes 2359300
  98.0 26.4 %all-to-all-start.1 = ((bf16[4,1,8,16,2048]{4,3,2,1,0:T(8,128)(2,1)}), bf16[4,1,8,16,2048]{4,3,2,1,0:T(8,128)(2,1)}, u32[]{:S(2)}, u32[]{:S(2)}) async-start(bf16[4,1,8,16,2048]{4,3,2,1,0:T(8,128)(2,1)} %bitcast.165), calls=%async_computation.1 | async-start | bytes 4194304 | tf_op jit(solution)/shard_map/all_to_all | solution.py:136
  102.5 149.8 %reduce-scatter.5.cloned.1.call-start = ((), (), s32[]{:S(2)}) async-start(), calls=%async_computation.7 | async-start | bytes 3538944 | tf_op jit(solution)/shard_map/reduce_scatter | solution.py:172
  132.4 24.7 %copy-start.9 = (bf16[512,768]{1,0:T(8,128)(2,1)S(1)}, bf16[512,768]{1,0:T(8,128)(2,1)}, u32[]{:S(2)}) copy-start(bf16[512,768]{1,0:T(8,128)(2,1)} %copy-done.8) | copy-start | bytes 2359300
  160.6 93.7 %reduce-scatter.3.cloned.1.call-start = ((), (), s32[]{:S(2)}) async-start(), calls=%async_computation.6 | async-start | bytes 7077888 | tf_op jit(solution)/shard_map/reduce_scatter | solution.py:169
  160.9 6.0 %copy-start.6 = (bf16[4,1,8,16,2048]{4,3,2,1,0:T(8,128)(2,1)S(1)}, bf16[4,1,8,16,2048]{4,3,2,1,0:T(8,128)(2,1)}, u32[]{:S(2)}) copy-start(bf16[4,1,8,16,2048]{4,3,2,1,0:T(8,128)(2,1)} %copy-done.5) | copy-start | bytes 6291460
  172.6 1.4 copy-start.15
  181.5 24.5 %all-to-all-start.3 = ((bf16[4,1,8,16,2048]{4,3,2,1,0:T(8,128)(2,1)}), bf16[4,1,8,16,2048]{4,3,2,1,0:T(8,128)(2,1)}, u32[]{:S(2)}, u32[]{:S(2)}) async-start(bf16[4,1,8,16,2048]{4,3,2,1,0:T(8,128)(2,1)} %bitcast.34), calls=%async_computation.3 | async-start | bytes 4194304 | tf_op jit(solution)/shard_map/all_to_all | solution.py:146
  214.2 9.3 %copy-start.2 = (f32[8,32,4120]{2,1,0:T(8,128)S(1)}, f32[8,32,4120]{2,1,0:T(8,128)}, u32[]{:S(2)}) copy-start(f32[8,32,4120]{2,1,0:T(8,128)} %concatenate.22) | copy-start | bytes 12656644
  217.0 6.5 %collective-permute-start.7 = (bf16[32,4120]{1,0:T(8,128)(2,1)S(1)}, bf16[32,4120]{1,0:T(8,128)(2,1)S(1)}, u32[]{:S(2)}, u32[]{:S(2)}) collective-permute-start(bf16[32,4120]{1,0:T(8,128)(2,1)S(1)} %get-tuple-element.44), channel_id=1, source_target_pairs={{0,7},{1,0},{2,1},{3,2},{4,3},{5,4},{6,5},{7,6},{8,15},{9,8},{10,9... | collective-permute-start | bytes 791048 | tf_op jit(solution)/shard_map/ppermute | solution.py:58
  218.4 8.8 %collective-permute-start.11 = (bf16[32,4120]{1,0:T(8,128)(2,1)S(1)}, bf16[32,4120]{1,0:T(8,128)(2,1)S(1)}, u32[]{:S(2)}, u32[]{:S(2)}) collective-permute-start(bf16[32,4120]{1,0:T(8,128)(2,1)S(1)} %get-tuple-element.45), channel_id=1, source_target_pairs={{0,1},{1,2},{2,3},{3,4},{4,5},{5,6},{6,7},{7,0},{8,9},{9,10},{10,1... | collective-permute-start | bytes 791048 | tf_op jit(solution)/shard_map/ppermute | solution.py:58
  223.6 7.8 %collective-permute-start.8 = (bf16[32,4120]{1,0:T(8,128)(2,1)S(1)}, bf16[32,4120]{1,0:T(8,128)(2,1)S(1)}, u32[]{:S(2)}, u32[]{:S(2)}) collective-permute-start(bf16[32,4120]{1,0:T(8,128)(2,1)S(1)} %fusion.50), channel_id=1, source_target_pairs={{0,7},{1,0},{2,1},{3,2},{4,3},{5,4},{6,5},{7,6},{8,15},{9,8},{10,9... | collective-permute-start | bytes 791048 | tf_op jit(solution)/shard_map/ppermute | solution.py:58
  231.4 8.8 %collective-permute-start.9 = (bf16[32,4120]{1,0:T(8,128)(2,1)S(1)}, bf16[32,4120]{1,0:T(8,128)(2,1)S(1)}, u32[]{:S(2)}, u32[]{:S(2)}) collective-permute-start(bf16[32,4120]{1,0:T(8,128)(2,1)S(1)} %get-tuple-element.42), channel_id=1, source_target_pairs={{0,7},{1,0},{2,1},{3,2},{4,3},{5,4},{6,5},{7,6},{8,15},{9,8},{10,9... | collective-permute-start | bytes 791048 | tf_op jit(solution)/shard_map/ppermute | solution.py:58
  235.2 7.7 %collective-permute-start.12 = (bf16[32,4120]{1,0:T(8,128)(2,1)S(1)}, bf16[32,4120]{1,0:T(8,128)(2,1)S(1)}, u32[]{:S(2)}, u32[]{:S(2)}) collective-permute-start(bf16[32,4120]{1,0:T(8,128)(2,1)S(1)} %get-tuple-element.43), channel_id=1, source_target_pairs={{0,1},{1,2},{2,3},{3,4},{4,5},{5,6},{6,7},{7,0},{8,9},{9,10},{10,1... | collective-permute-start | bytes 791048 | tf_op jit(solution)/shard_map/ppermute | solution.py:58
  243.0 6.5 %collective-permute-start.10 = (bf16[32,4120]{1,0:T(8,128)(2,1)S(1)}, bf16[32,4120]{1,0:T(8,128)(2,1)S(1)}, u32[]{:S(2)}, u32[]{:S(2)}) collective-permute-start(bf16[32,4120]{1,0:T(8,128)(2,1)S(1)} %get-tuple-element.40), channel_id=1, source_target_pairs={{0,7},{1,0},{2,1},{3,2},{4,3},{5,4},{6,5},{7,6},{8,15},{9,8},{10,9... | collective-permute-start | bytes 791048 | tf_op jit(solution)/shard_map/ppermute | solution.py:58
  243.0 7.7 %collective-permute-start.13 = (bf16[32,4120]{1,0:T(8,128)(2,1)S(1)}, bf16[32,4120]{1,0:T(8,128)(2,1)S(1)}, u32[]{:S(2)}, u32[]{:S(2)}) collective-permute-start(bf16[32,4120]{1,0:T(8,128)(2,1)S(1)} %get-tuple-element.41), channel_id=1, source_target_pairs={{0,1},{1,2},{2,3},{3,4},{4,5},{5,6},{6,7},{7,0},{8,9},{9,10},{10,1... | collective-permute-start | bytes 791048 | tf_op jit(solution)/shard_map/ppermute | solution.py:58
  250.8 6.0 %copy-start.1 = (bf16[1,768,2048]{2,1,0:T(8,128)(2,1)S(1)}, bf16[1,768,2048]{2,1,0:T(8,128)(2,1)}, u32[]{:S(2)}) copy-start(bf16[1,768,2048]{2,1,0:T(8,128)(2,1)} %param.11) | copy-start | bytes 9437188
  (4 other events, 4.5 us)
Sparse Core Ops, SparseCore 0:
  160.7 31.9 reduce-scatter.4
  195.3 45.5 reduce-scatter.2
